TPU v7x, 32 devices: a whole 2x2x4 slice. The times are simulated.
32 devices in a mesh: rep: 4 (over x, core), frame: 4 (over z), row: 2 (over y).
Axes of the slice: x: 2, y: 2, z: 4, core: 2. Of those that a mesh axis runs over, the one named last changes fastest.
Arguments:
- activations: bfloat16 [4, 4, 16, 32, 1280], P('rep', 'frame', 'row'), may hold values from -70 to 70, as said below
- spatial_weight: bfloat16 [9, 1280, 1280], P(None, None, ('rep', 'frame')), may hold values from -0.0546875 to 0.0546875
- temporal_weight: bfloat16 [3, 1280, 1280], P(None, None, ('rep', 'frame')), may hold values from -0.09375 to 0.09375
- first_gain: float32 [1280], replicated, may hold values from 0.25 to 1.75
- first_shift: float32 [1280], replicated, may hold values from -1.5 to 1.5
- spatial_bias: float32 [1280], replicated, may hold values from -2.5 to 2.5
- second_gain: float32 [1280], replicated, may hold values from 0.25 to 1.75
- second_shift: float32 [1280], replicated, may hold values from -1.5 to 1.5
- temporal_bias: float32 [1280], replicated, may hold values from -1.5 to 1.5
Outputs:
- block_out: float32 [4, 4, 16, 32, 1280], P('rep', 'frame', 'row')
Inputs may be any that keep to these rules, and one draw needn't show every extreme that they name: `activations`: finite values.
All inputs are finite; a program needn't handle non-finite values.
Results may differ from a plain program's by a relative error of at most 0.0009.
Values may be sent and summed in bfloat16 or wider, within the bound.
No kernel may reach another device: no remote copies, remote signals or barrier semaphores. Data moves between devices by JAX's collectives and lax.ppermute only.
A program may use at most 128 MiB of HBM per device.

v0:
```python
import numpy as np
import jax
import jax.numpy as jnp
from jax import lax
from jax.sharding import PartitionSpec as P

GROUPS = 32
EPS = 1e-05


def pair_sum(value, axis):
    if lax.axis_size(axis) == 2:
        return jax.tree.map(lambda v: v + lax.ppermute(v, axis, [(0, 1), (1, 0)]), value)
    return lax.psum(value, axis)


def gather_rep(w):
    size = lax.axis_size("rep")
    if size & size - 1 != 0:
        return (lax.all_gather(w, "rep", axis=w.ndim - 1, tiled=True), list(range(size)))
    index = lax.axis_index("rep")
    blocks = w[None]
    order = [0]
    step = size // 2
    while step >= 1:
        recv = lax.ppermute(blocks, "rep", [(k, k ^ step) for k in range(size)])
        upper = index & step != 0
        low = jnp.where(upper, recv, blocks)
        high = jnp.where(upper, blocks, recv)
        blocks = jnp.concatenate([low, high], axis=0)
        order = order + [o + step for o in order]
        step //= 2
    out = jnp.moveaxis(blocks, 0, -2)
    return (out.reshape(out.shape[:-2] + (-1,)), order)


def local_vector(vec, order, frame_index, rep_size, frame_size):
    width = vec.shape[0] // (rep_size * frame_size)
    table = vec.reshape(rep_size, frame_size, width)[np.array(order)]
    return lax.dynamic_index_in_dim(table, frame_index, axis=1, keepdims=False).reshape(-1)


def silu_bf16(normed):
    return jax.nn.silu(normed).astype(jnp.bfloat16)


def shards(
    activations,
    spatial_weight,
    temporal_weight,
    first_gain,
    first_shift,
    spatial_bias,
    second_gain,
    second_shift,
    temporal_bias,
):
    rep_size = lax.axis_size("rep")
    frame_size = lax.axis_size("frame")
    row_size = lax.axis_size("row")
    frame_index = lax.axis_index("frame")
    row_index = lax.axis_index("row")
    channels = activations.shape[-1]
    rows = activations.shape[2]
    cols = activations.shape[3]
    width = channels // GROUPS
    shard_width = spatial_weight.shape[-1]
    spatial_w, order = gather_rep(spatial_weight)
    temporal_w, _ = gather_rep(temporal_weight)
    local = spatial_w.shape[-1]
    raw = lax.all_gather(activations, "frame", axis=1, tiled=True)
    frames = raw.shape[1]
    if row_size > 1:
        down = [(i, i + 1) for i in range(row_size - 1)]
        up = [(i + 1, i) for i in range(row_size - 1)]
        above = lax.ppermute(raw[:, :, rows - 1 :], "row", down)
        below = lax.ppermute(raw[:, :, :1], "row", up)
    else:
        above = jnp.zeros_like(raw[:, :, :1])
        below = jnp.zeros_like(raw[:, :, :1])
    inputs = raw.astype(jnp.float32)
    grouped = inputs.reshape(1, -1, GROUPS, width)
    sums = jnp.sum(grouped, axis=(1, 3))
    squares = jnp.sum(grouped * grouped, axis=(1, 3))
    sums, squares = pair_sum((sums, squares), "row")
    count = grouped.shape[1] * width * row_size
    mean = sums / count
    variance = squares / count - mean * mean
    inverse = lax.rsqrt(variance + EPS)
    mean_full = jnp.repeat(mean, width, axis=1)[:, None, None, None, :]
    inverse_full = jnp.repeat(inverse, width, axis=1)[:, None, None, None, :]

    def first_norm(x):
        normed = (x.astype(jnp.float32) - mean_full) * inverse_full * first_gain + first_shift
        return silu_bf16(normed)

    first_mid = first_norm(raw)
    first_above = jnp.where(row_index > 0, first_norm(above), jnp.zeros((), jnp.bfloat16))
    first_below = jnp.where(
        row_index < row_size - 1, first_norm(below), jnp.zeros((), jnp.bfloat16)
    )
    padded = jnp.concatenate([first_above, first_mid, first_below], axis=2)
    lhs = padded.reshape(frames, rows + 2, cols, channels)
    kernel = spatial_w.reshape(3, 3, channels, local)
    spatial = lax.conv_general_dilated(
        lhs,
        kernel,
        window_strides=(1, 1),
        padding=((0, 0), (1, 1)),
        dimension_numbers=("NHWC", "HWIO", "NHWC"),
        preferred_element_type=jnp.float32,
    )
    spatial = spatial + local_vector(spatial_bias, order, frame_index, rep_size, frame_size)
    g2 = local_vector(second_gain, order, frame_index, rep_size, frame_size)
    s2 = local_vector(second_shift, order, frame_index, rep_size, frame_size)
    if shard_width % width == 0:
        grouped2 = spatial.reshape(-1, local // width, width)
        sums2 = jnp.sum(grouped2, axis=(0, 2))
        squares2 = jnp.sum(grouped2 * grouped2, axis=(0, 2))
        sums2, squares2 = pair_sum((sums2, squares2), "row")
        count2 = grouped2.shape[0] * width * row_size
        mean2 = sums2 / count2
        variance2 = squares2 / count2 - mean2 * mean2
        inverse2 = lax.rsqrt(variance2 + EPS)
        mean2_full = jnp.repeat(mean2, width)
        inverse2_full = jnp.repeat(inverse2, width)
    else:
        flat = spatial.reshape(-1, local)
        csum = jnp.sum(flat, axis=0)
        csq = jnp.sum(flat * flat, axis=0)
        csum, csq = pair_sum((csum, csq), "row")
        both = lax.all_gather(jnp.stack([csum, csq]), "frame", axis=0)
        both = both.reshape(frame_size, 2, rep_size, shard_width)
        inv_order = np.argsort(np.array(order))
        both = both[:, :, inv_order]
        both = jnp.transpose(both, (1, 2, 0, 3)).reshape(2, GROUPS, -1)
        gsum = jnp.sum(both, axis=2)
        count2 = flat.shape[0] * row_size * width
        gmean = gsum[0] / count2
        gvar = gsum[1] / count2 - gmean * gmean
        ginv = lax.rsqrt(gvar + EPS)
        mean2_full = local_vector(
            jnp.repeat(gmean, width), order, frame_index, rep_size, frame_size
        )
        inverse2_full = local_vector(
            jnp.repeat(ginv, width), order, frame_index, rep_size, frame_size
        )
    second = silu_bf16((spatial - mean2_full) * inverse2_full * g2 + s2)
    second_all = lax.all_gather(second, "frame", axis=3, tiled=True)
    rows_order = np.arange(channels).reshape(rep_size, frame_size, shard_width)
    rows_order = rows_order[np.array(order)].transpose(1, 0, 2).reshape(-1)
    temporal_w = temporal_w[:, rows_order, :]
    lhs_t = second_all.reshape(frames, rows * cols, frame_size * local)[None]
    kernel_t = temporal_w.reshape(3, 1, frame_size * local, local)
    temporal = lax.conv_general_dilated(
        lhs_t,
        kernel_t,
        window_strides=(1, 1),
        padding=((1, 1), (0, 0)),
        dimension_numbers=("NHWC", "HWIO", "NHWC"),
        preferred_element_type=jnp.float32,
    )
    temporal = temporal.reshape(1, frames, rows, cols, local).astype(jnp.bfloat16)
    back = lax.all_to_all(temporal, "frame", split_axis=1, concat_axis=4, tiled=True)
    per_frame = frames // frame_size
    back = back.reshape(1, per_frame, rows, cols, frame_size, rep_size, shard_width)
    back = back[:, :, :, :, :, np.argsort(np.array(order))]
    back = jnp.swapaxes(back, 4, 5).reshape(1, per_frame, rows, cols, channels)
    return activations.astype(jnp.float32) + back.astype(jnp.float32) + temporal_bias


def solution(mesh):
    placed = (
        P("rep", "frame", "row", None, None),
        P(None, None, ("rep", "frame")),
        P(None, None, ("rep", "frame")),
        P(),
        P(),
        P(),
        P(),
        P(),
        P(),
    )
    return jax.shard_map(
        shards,
        mesh=mesh,
        in_specs=placed,
        out_specs=P("rep", "frame", "row", None, None),
        check_vma=False,
    )
```

profile of v0, /device:TPU:0, one launch (start us, length us, event | category | flops | bytes accessed | tf_op | source)
XLA Modules:
  0.0 381.3 jit_solution(2174034292066160613)
XLA Ops:
  7.3 3.0 collective-permute-start.4
  15.4 35.5 %collective-permute-done.4 = bf16[1,9,1280,80]{2,3,1,0:T(8,128)(2,1)} collective-permute-done((bf16[1,9,1280,80]{2,3,1,0:T(8,128)(2,1)}, bf16[1,9,1280,80]{2,3,1,0:T(8,128)(2,1)}, u32[]{:S(2)}, u32[]{:S(2)}) %collective-permute-start.4) | collective-permute-done | bytes 1843232 | tf_op jit(solution)/shard_map/ppermute | solution.py:26
  50.8 2.3 broadcast_select_fusion.3
  53.2 2.4 pad_maximum_fusion
  55.6 10.8 %all-gather.3.cloned.1.call-done = bf16[1,4,8,32,1280]{4,3,2,0,1:T(8,128)(2,1)} async-done(((bf16[1,1,8,32,1280]{4,3,2,0,1:T(8,128)(2,1)}), bf16[1,4,8,32,1280]{4,3,2,0,1:T(8,128)(2,1)}) %all-gather.3.cloned.1.call-update) | async-done | bytes 2621456 | tf_op jit(solution)/shard_map/all_gather | solution.py:71
  67.5 3.4 collective-permute-start
  70.9 2.5 convert_reduce_fusion
  73.9 2.1 collective-permute-start.2
  78.1 3.5 fusion.14
  81.7 4.6 %collective-permute-done.3 = bf16[1,4,1,32,1280]{4,3,2,0,1:T(8,128)(2,1)S(1)} collective-permute-done((bf16[1,4,1,32,1280]{4,3,2,0,1:T(8,128)(2,1)S(1)}, bf16[1,4,1,32,1280]{4,3,2,0,1:T(8,128)(2,1)S(1)}, u32[]{:S(2)}, u32[]{:S(2)}) %collective-permute-start.3) | collective-permute-done | bytes 327712 | tf_op jit(solution)/shard_map/ppermute | solution.py:77
  87.2 2.5 copy.78
  89.7 1.6 pad.clone
  91.9 4.8 %fusion.1 = bf16[10,4,8,7,1280]{4,1,3,2,0:T(4,128)(2,1)} fusion(bf16[10,4,7,2,1280]{4,1,3,2,0:T(4,128)(2,1)S(1)} %slice.23, bf16[10,4,8,5,1280]{4,1,3,2,0:T(4,128)(2,1)S(1)} %bitcast.63), kind=kLoop, calls=%fused_computation.11 | loop fusion | flops 17203200 | bytes 11264000 | tf_op jit(solution)/shard_map/conv_general_dilated | solution.py:105
  96.7 4.7 %broadcast_select_fusion.1 = (bf16[2,9,1280,80]{2,3,1,0:T(8,128)(2,1)}, bf16[2,9,1280,80]{2,3,1,0:T(8,128)(2,1)}) fusion(bf16[2,9,1280,80]{2,3,1,0:T(8,128)(2,1)} %collective-permute-done.5, pred[]{:T(512)S(6)} %ne.8, bf16[1,9,1280,80]{2,3,1,0:T(8,128)(2,1)S(1)} %copy-done.1, bf16[1,9,1280,80]{2,3,1,0:T(8,128)(2,1)S(1)} %get-tuple-element.13), kind=kLoop, calls=%fused_computation.27 | loop fusion | flops 5529600 | bytes 14745601 | tf_op jit(solution)/shard_map/jit(_where)/select_n | solution.py:28
  101.5 6.8 %maximum_bitcast_fusion = bf16[9,1280,4,80]{1,3,0,2:T(8,128)(2,1)} fusion(bf16[2,9,1280,80]{2,3,1,0:T(8,128)(2,1)} %get-tuple-element.12, bf16[2,9,1280,80]{2,3,1,0:T(8,128)(2,1)} %get-tuple-element.11), kind=kLoop, calls=%fused_computation.10 | loop fusion | flops 3686400 | bytes 14745600 | tf_op jit(solution)/shard_map/transpose | solution.py:33
  108.2 3.8 copy.66
  112.0 17.7 %select_reduce_fusion = (f32[320]{0:T(512)S(1)}, f32[320]{0:T(512)S(1)}, f32[8,32,5,320]{3,1,2,0:T(8,128)S(1)}) fusion(pred[32,5]{0,1:T(8,128)(4,1)S(1)} %copy-done.7, f32[320]{0:T(512)S(1)} %add.127, bf16[3,3,1280,320]{2,3,1,0:T(8,128)(2,1)S(1)} %bitcast.65, bf16[10,4,8,7,1280]{4,1,3,2,0:T(4,128)(2,1)} %fusion.1), kind=kOutput, calls=%fused_computation.34 | convolution fusion | flops 9440051200 | bytes 14749600 | tf_op jit(solution)/shard_map/conv_general_dilated | solution.py:105
  130.2 2.1 collective-permute-start.6
  132.3 1.3 collective-permute-done.7
  135.2 5.4 %copy.68 = bf16[4,8,32,320]{2,1,0,3:T(8,128)(2,1)} copy(bf16[4,8,32,320]{3,1,2,0:T(8,128)(2,1)S(1)} %slice_bitcast_fusion) | data formatting | bytes 1310720 | tf_op jit(solution)/shard_map/convert_element_type | solution.py:44
  140.7 1.5 collective-permute-start.8
  142.3 11.1 %collective-permute-done.8 = bf16[1,3,1280,80]{2,3,0,1:T(8,128)(2,1)S(1)} collective-permute-done((bf16[1,3,1280,80]{2,3,0,1:T(8,128)(2,1)S(1)}, bf16[1,3,1280,80]{2,3,0,1:T(8,128)(2,1)S(1)}, u32[]{:S(2)}, u32[]{:S(2)}) %collective-permute-start.8) | collective-permute-done | bytes 614432 | tf_op jit(solution)/shard_map/ppermute | solution.py:26
  153.7 2.9 collective-permute-done.9
  157.0 6.3 %copy.69 = bf16[3,1280,320]{2,0,1:T(4,128)(2,1)} copy(bf16[3,1280,320]{1,2,0:T(8,128)(2,1)S(1)} %bitcast.64) | data formatting | bytes 4915200 | tf_op jit(solution)/shard_map/reshape | solution.py:34
  163.3 12.0 %gather_fusion.3 = bf16[1280,3,320]{2,1,0:T(4,128)(2,1)} fusion(bf16[3,1280,320]{2,0,1:T(4,128)(2,1)} %copy.69, s32[2048]{0:T(1024)S(1)} %pad_clamp_fusion), kind=kCustom, calls=%fused_computation.3 | custom fusion | bytes 4920320 | tf_op jit(solution)/shard_map/gather | solution.py:152
  175.4 148.9 %all-gather.5.cloned.1.call-done = bf16[4,8,32,1280]{2,1,0,3:T(8,128)(2,1)} async-done(((bf16[4,8,32,320]{2,1,0,3:T(8,128)(2,1)}), bf16[4,8,32,1280]{2,1,0,3:T(8,128)(2,1)}) %all-gather.5.cloned.1.call-update) | async-done | bytes 2621456 | tf_op jit(solution)/shard_map/all_gather | solution.py:149
  324.3 12.8 %copy.70 = bf16[4,8,32,1280]{3,1,2,0:T(8,128)(2,1)S(1)} copy(bf16[4,8,32,1280]{2,1,0,3:T(8,128)(2,1)} %all-gather.5.cloned.1.call-done) | data formatting | bytes 5242880 | tf_op jit(solution)/shard_map/all_gather | solution.py:149
  337.1 6.3 %fusion.22 = bf16[1,4,8,32,320]{4,2,3,0,1:T(8,128)(2,1)S(1)} fusion(bf16[4,8,32,1280]{3,1,2,0:T(8,128)(2,1)S(1)} %copy.70, bf16[3,1,1280,320]{3,0,2,1:T(4,128)(2,1)} %bitcast.69), kind=kOutput, calls=%fused_computation.41 | convolution fusion | flops 2097479680 | bytes 5734400 | tf_op jit(solution)/shard_map/conv_general_dilated | solution.py:155
  343.5 23.0 %all_to_all.15 = bf16[1,4,8,32,320]{4,2,3,0,1:T(8,128)(2,1)S(1)} all-to-all(bf16[1,4,8,32,320]{4,2,3,0,1:T(8,128)(2,1)S(1)} %fusion.22), channel_id=1, replica_groups=mesh['rep'=4,'frame'=4,'row'=2] {'frame'}, dimensions={1} | all-to-all | bytes 1310720 | tf_op jit(solution)/shard_map/all_to_all | solution.py:164
  368.5 1.4 copy.75
  369.9 2.2 reshape.124
  372.2 2.3 add_add_fusion
  (76 shorter events, 15.8 us)
Async XLA Ops:
  6.5 59.9 %all-gather.3.cloned.1.call-start = ((), (), s32[]{:S(2)}) async-start(), calls=%async_computation.1 | async-start | bytes 3276800 | tf_op jit(solution)/shard_map/all_gather | solution.py:71
  7.3 317.0 %all-gather.5.cloned.1.call-start = ((), (), s32[]{:S(2)}) async-start(), calls=%async_computation.2 | async-start | bytes 13107200 | tf_op jit(solution)/shard_map/all_gather | solution.py:149
  7.3 43.5 %collective-permute-start.4 = (bf16[1,9,1280,80]{2,3,1,0:T(8,128)(2,1)}, bf16[1,9,1280,80]{2,3,1,0:T(8,128)(2,1)}, u32[]{:S(2)}, u32[]{:S(2)}) collective-permute-start(bf16[1,9,1280,80]{2,3,1,0:T(8,128)(2,1)} %bitcast.70), channel_id=1, source_target_pairs={{0,16},{8,24},{16,0},{24,8},{1,17},{9,25},{17,1},{25,9},{2,18},{10... | collective-permute-start | bytes 5529608 | tf_op jit(solution)/shard_map/ppermute | solution.py:26
  53.1 2.4 copy-start
  55.6 22.5 %copy-start.3 = (f32[1280]{0:T(1024)S(1)}, f32[1280]{0:T(1024)}, u32[]{:S(2)}) copy-start(f32[1280]{0:T(1024)} %param.23) | copy-start | bytes 15364
  55.6 22.5 %copy-start.4 = (f32[1280]{0:T(1024)S(1)}, f32[1280]{0:T(1024)}, u32[]{:S(2)}) copy-start(f32[1280]{0:T(1024)} %param.22) | copy-start | bytes 15364
  55.6 41.2 %collective-permute-start.5 = (bf16[2,9,1280,80]{2,3,1,0:T(8,128)(2,1)}, bf16[2,9,1280,80]{2,3,1,0:T(8,128)(2,1)}, u32[]{:S(2)}, u32[]{:S(2)}) collective-permute-start(bf16[2,9,1280,80]{2,3,1,0:T(8,128)(2,1)} %pad_maximum_fusion), channel_id=1, source_target_pairs={{0,8},{8,0},{16,24},{24,16},{1,9},{9,1},{17,25},{25,17},{2,10},{10... | collective-permute-start | bytes 11059208 | tf_op jit(solution)/shard_map/ppermute | solution.py:26
  67.5 14.1 %collective-permute-start = (bf16[1,4,1,32,1280]{4,3,2,0,1:T(8,128)(2,1)S(1)}, bf16[1,4,1,32,1280]{4,3,2,0,1:T(8,128)(2,1)S(1)}, u32[]{:S(2)}, u32[]{:S(2)}) collective-permute-start(bf16[1,4,1,32,1280]{4,3,2,0,1:T(8,128)(2,1)S(1)} %get-tuple-element.15), channel_id=1, source_target_pairs={{0,1},{2,3},{4,5},{6,7},{8,9},{10,11},{12,13},{14,15},{16,17},{18,... | collective-permute-start | bytes 983048 | tf_op jit(solution)/shard_map/ppermute | solution.py:76
  73.6 4.1 %collective-permute-start.1 = (f32[1,32]{1,0:T(1,128)S(1)}, f32[1,32]{1,0:T(1,128)S(1)}, u32[]{:S(2)}, u32[]{:S(2)}) collective-permute-start(f32[1,32]{1,0:T(1,128)S(1)} %bitcast.72), channel_id=1, source_target_pairs={{0,1},{1,0},{2,3},{3,2},{4,5},{5,4},{6,7},{7,6},{8,9},{9,8},{10,11... | collective-permute-start | bytes 392 | tf_op jit(solution)/shard_map/ppermute | solution.py:13
  73.9 3.9 %collective-permute-start.2 = (f32[1,32]{1,0:T(1,128)S(1)}, f32[1,32]{1,0:T(1,128)S(1)}, u32[]{:S(2)}, u32[]{:S(2)}) collective-permute-start(f32[1,32]{1,0:T(1,128)S(1)} %bitcast.73), channel_id=1, source_target_pairs={{0,1},{1,0},{2,3},{3,2},{4,5},{5,4},{6,7},{7,6},{8,9},{9,8},{10,11... | collective-permute-start | bytes 392 | tf_op jit(solution)/shard_map/ppermute | solution.py:13
  76.0 10.3 %collective-permute-start.3 = (bf16[1,4,1,32,1280]{4,3,2,0,1:T(8,128)(2,1)S(1)}, bf16[1,4,1,32,1280]{4,3,2,0,1:T(8,128)(2,1)S(1)}, u32[]{:S(2)}, u32[]{:S(2)}) collective-permute-start(bf16[1,4,1,32,1280]{4,3,2,0,1:T(8,128)(2,1)S(1)} %get-tuple-element.16), channel_id=1, source_target_pairs={{1,0},{3,2},{5,4},{7,6},{9,8},{11,10},{13,12},{15,14},{17,16},{19,... | collective-permute-start | bytes 983048 | tf_op jit(solution)/shard_map/ppermute | solution.py:77
  91.9 4.8 %copy-start.1 = (bf16[1,9,1280,80]{2,3,1,0:T(8,128)(2,1)S(1)}, bf16[1,9,1280,80]{2,3,1,0:T(8,128)(2,1)}, u32[]{:S(2)}) copy-start(bf16[1,9,1280,80]{2,3,1,0:T(8,128)(2,1)} %copy-done) | copy-start | bytes 5529604
  108.2 3.8 copy-start.7
  129.9 3.6 collective-permute-start.7
  130.2 3.6 collective-permute-start.6
  135.2 5.5 %copy-start.2 = (bf16[3,1280,80]{1,2,0:T(8,128)(2,1)S(1)}, bf16[3,1280,80]{1,2,0:T(8,128)(2,1)}, u32[]{:S(2)}) copy-start(bf16[3,1280,80]{1,2,0:T(8,128)(2,1)} %param.21) | copy-start | bytes 1843204
  140.7 13.0 %copy-start.6 = (s32[1280]{0:T(1024)S(1)}, s32[1280]{0:T(1024)}, u32[]{:S(2)}) copy-start(s32[1280]{0:T(1024)} %constant.82) | copy-start | bytes 15364
  140.7 12.6 %collective-permute-start.8 = (bf16[1,3,1280,80]{2,3,0,1:T(8,128)(2,1)S(1)}, bf16[1,3,1280,80]{2,3,0,1:T(8,128)(2,1)S(1)}, u32[]{:S(2)}, u32[]{:S(2)}) collective-permute-start(bf16[1,3,1280,80]{2,3,0,1:T(8,128)(2,1)S(1)} %bitcast.71), channel_id=1, source_target_pairs={{0,16},{8,24},{16,0},{24,8},{1,17},{9,25},{17,1},{25,9},{2,18},{10... | collective-permute-start | bytes 1843208 | tf_op jit(solution)/shard_map/ppermute | solution.py:26
  153.6 3.0 collective-permute-start.9
  369.9 2.3 copy-start.5
Sparse Core Ops, SparseCore 0:
  8.9 57.4 all-gather.2
  140.8 183.4 all-gather.4
where the time goes:
time: 382 us; the launch traced here: 381 us
  waiting for transfers between devices  217 us (57%)
  local copies, waits for them, and re-layouts  57.4 us (15%)
  other arithmetic  32.9 us (9%)
  matrix products  24 us (6%)
  blocking collectives  23 us (6%)
  between operations  13.7 us (4%)
  starting transfers between devices  13.6 us (4%)
    all_gather x1, waiting for transfers between devices, shards(): second_all = lax.all_gather(second, 'frame', axis=3, tiled=True)  149 us
    ppermute x4, waiting for transfers between devices, gather_rep(): recv = lax.ppermute(blocks, 'rep', [(k, k ^ step) for k in range(size)])  49.5 us
    all_to_all x1, blocking collectives, shards(): lax.all_to_all(temporal, 'frame', split_axis=1, concat_axis=4, tiled=True)  23 us
    conv_general_dilated x1, matrix products, shards(): lax.conv_general_dilated(lhs, kernel, window_strides=(1, 1), padding=((0,...  17.7 us
    all_gather x1, local copies, waits for them, and re-layouts, shards(): second_all = lax.all_gather(second, 'frame', axis=3, tiled=True)  12.8 us
    gather x1, local copies, waits for them, and re-layouts, shards(): temporal_w = temporal_w[:, rows_order, :]  12 us
    all_gather x1, waiting for transfers between devices, shards(): raw = lax.all_gather(activations, 'frame', axis=1, tiled=True)  10.8 us
  transfers between devices with their start and end apart: 12, of which 9 were waited for; matrix products, arithmetic and copies ran while one was open for 12% of the time, Pallas kernels for 0%

commit v1 on v0

--- a/solution.py
+++ b/solution.py
@@ -6,6 +6,19 @@
 
 GROUPS = 32
 EPS = 1e-05
+
+
+def return_all_shifts_all_here(vector):
+    bus_axis = "frame"
+    block_now, local_next = (lax.axis_size(bus_axis), lax.axis_index(bus_axis))
+    m_next, out_arr = (vector, 1)
+    while out_arr < block_now:
+        carry = lax.ppermute(m_next, bus_axis, [(s, s ^ out_arr) for s in range(block_now)])
+        z_new = jnp.concatenate([m_next, carry], axis=3)
+        o_now = jnp.concatenate([carry, m_next], axis=3)
+        m_next = jnp.where(local_next & out_arr == 0, z_new, o_now)
+        out_arr = 2 * out_arr
+    return m_next
 
 
 def pair_sum(value, axis):
@@ -146,7 +159,7 @@
             jnp.repeat(ginv, width), order, frame_index, rep_size, frame_size
         )
     second = silu_bf16((spatial - mean2_full) * inverse2_full * g2 + s2)
-    second_all = lax.all_gather(second, "frame", axis=3, tiled=True)
+    second_all = return_all_shifts_all_here(second)
     rows_order = np.arange(channels).reshape(rep_size, frame_size, shard_width)
     rows_order = rows_order[np.array(order)].transpose(1, 0, 2).reshape(-1)
     temporal_w = temporal_w[:, rows_order, :]

time: 382 us -> 268 us (0.70)
  waiting for transfers between devices: 217 us -> 104 us
  local copies, waits for them, and re-layouts: 57.4 us -> 42.2 us
  other arithmetic: 32.9 us -> 42.7 us
    all_gather x1 -> x0, waiting for transfers between devices: 149 us -> none  [shards(): second_all = lax.all_gather(second, 'frame', axis=3, tiled=True)]
    ppermute x0 -> x2, waiting for transfers between devices: none -> 47.4 us  [return_all_shifts_all_here(): lax.ppermute(m_next, bus_axis, [(s, s ^ out_arr) for s in range(block_now)])]
    all_gather x1 -> x0, local copies, waits for them, and re-layouts: 12.8 us -> none  [shards(): second_all = lax.all_gather(second, 'frame', axis=3, tiled=True)]
    all_gather x1, waiting for transfers between devices: 10.8 us -> 0.01 us  [shards(): raw = lax.all_gather(activations, 'frame', axis=1, tiled=True)]
    convert_element_type x3, local copies, waits for them, and re-layouts: 5.86 us -> 0.52 us  [silu_bf16(): return jax.nn.silu(normed).astype(jnp.bfloat16)]
    ppermute x0 -> x2, starting transfers between devices: none -> 4.23 us  [return_all_shifts_all_here(): lax.ppermute(m_next, bus_axis, [(s, s ^ out_arr) for s in range(block_now)])]
  transfers between devices with their start and end apart: 12 -> 13, of which waited for: 9 -> 7; matrix products, arithmetic and copies ran while one was open for 12% -> 34% of each run, Pallas kernels for 0% -> 0%
where the time goes in v1:
time: 268 us; the launch traced here: 267 us
  waiting for transfers between devices  104 us (39%)
  other arithmetic  42.7 us (16%)
  local copies, waits for them, and re-layouts  42.2 us (16%)
  blocking collectives  24.8 us (9%)
  matrix products  23 us (9%)
  starting transfers between devices  17.1 us (6%)
  between operations  13.8 us (5%)
    ppermute x4, waiting for transfers between devices, gather_rep(): recv = lax.ppermute(blocks, 'rep', [(k, k ^ step) for k in range(size)])  48.5 us
    ppermute x2, waiting for transfers between devices, return_all_shifts_all_here(): lax.ppermute(m_next, bus_axis, [(s, s ^ out_arr) for s in range(block_now)])  47.4 us
    all_to_all x1, blocking collectives, shards(): lax.all_to_all(temporal, 'frame', split_axis=1, concat_axis=4, tiled=True)  24.8 us
    conv_general_dilated x1, matrix products, shards(): lax.conv_general_dilated(lhs, kernel, window_strides=(1, 1), padding=((0,...  18.7 us
    gather x1, local copies, waits for them, and re-layouts, shards(): temporal_w = temporal_w[:, rows_order, :]  12 us
    select_n x4, other arithmetic, gather_rep(): low = jnp.where(upper, recv, blocks)  9.59 us
    transpose x1, other arithmetic, gather_rep(): out = jnp.moveaxis(blocks, 0, -2)  6.76 us
    reshape x1, local copies, waits for them, and re-layouts, gather_rep(): return (out.reshape(out.shape[:-2] + (-1,)), order)  6.23 us
  transfers between devices with their start and end apart: 13, of which 7 were waited for; matrix products, arithmetic and copies ran while one was open for 34% of the time, Pallas kernels for 0%

profile of v1, /device:TPU:0, one launch (start us, length us, event | category | flops | bytes accessed | tf_op | source)
XLA Modules:
  0.0 267.4 jit_solution(8811642105668890717)
XLA Ops:
  7.3 3.0 %collective-permute-start.4 = (bf16[1,9,1280,80]{2,3,1,0:T(8,128)(2,1)}, bf16[1,9,1280,80]{2,3,1,0:T(8,128)(2,1)}, u32[]{:S(2)}, u32[]{:S(2)}) collective-permute-start(bf16[1,9,1280,80]{2,3,1,0:T(8,128)(2,1)} %bitcast.79), channel_id=1, source_target_pairs={{0,16},{8,24},{16,0},{24,8},{1,17},{9,25},{17,1},{25,9},{2,18},{10... | collective-permute-start | bytes 5529608 | tf_op jit(solution)/shard_map/ppermute | solution.py:39
  15.4 48.5 %collective-permute-done.10 = bf16[1,3,1280,80]{2,3,0,1:T(8,128)(2,1)S(1)} collective-permute-done((bf16[1,3,1280,80]{2,3,0,1:T(8,128)(2,1)}, bf16[1,3,1280,80]{2,3,0,1:T(8,128)(2,1)S(1)}, u32[]{:S(2)}, u32[]{:S(2)}) %collective-permute-start.10) | collective-permute-done | bytes 614432 | tf_op jit(solution)/shard_map/ppermute | solution.py:39
  66.3 2.3 broadcast_select_fusion.3
  68.6 2.3 pad_maximum_fusion
  71.5 2.5 convert_reduce_fusion
  74.2 1.8 collective-permute-start.1
  77.7 3.7 %collective-permute-start = (bf16[1,4,1,32,1280]{4,3,2,0,1:T(8,128)(2,1)S(1)}, bf16[1,4,1,32,1280]{4,3,2,0,1:T(8,128)(2,1)S(1)}, u32[]{:S(2)}, u32[]{:S(2)}) collective-permute-start(bf16[1,4,1,32,1280]{4,3,2,0,1:T(8,128)(2,1)S(1)} %get-tuple-element.15), channel_id=1, source_target_pairs={{0,1},{2,3},{4,5},{6,7},{8,9},{10,11},{12,13},{14,15},{16,17},{18,... | collective-permute-start | bytes 983048 | tf_op jit(solution)/shard_map/ppermute | solution.py:89
  83.1 3.5 %fusion.14 = bf16[1,4,8,32,1280]{4,3,2,0,1:T(8,128)(2,1)S(1)} fusion(bf16[1,4,8,32,1280]{4,3,2,0,1:T(8,128)(2,1)} %all-gather.2.cloned.1.call-done, f32[1280]{0:T(1024)S(1)} %copy-done.7, f32[1280]{0:T(1024)S(1)} %copy-done.8, f32[1280]{0:T(1024)S(1)} %broadcast_in_dim.52, f32[1280]{0:T(1024)S(1)} %broadcast_in_dim.50), kind=kLoop, calls=%fused_computation.24 | loop fusion | flops 13107200 | bytes 5263360 | tf_op jit(solution)/shard_map/convert_element_type | solution.py:57
  87.9 4.2 %collective-permute-done.3 = bf16[1,4,1,32,1280]{4,3,2,0,1:T(8,128)(2,1)} collective-permute-done((bf16[1,4,1,32,1280]{4,3,2,0,1:T(8,128)(2,1)S(1)}, bf16[1,4,1,32,1280]{4,3,2,0,1:T(8,128)(2,1)}, u32[]{:S(2)}, u32[]{:S(2)}) %collective-permute-start.3) | collective-permute-done | bytes 327712 | tf_op jit(solution)/shard_map/ppermute | solution.py:90
  92.2 1.5 fusion.31
  94.1 2.5 copy.89
  96.6 1.6 pad.clone
  98.8 4.8 %fusion.1 = bf16[10,4,8,7,1280]{4,1,3,2,0:T(4,128)(2,1)} fusion(bf16[10,4,7,2,1280]{4,1,3,2,0:T(4,128)(2,1)S(1)} %slice.23, bf16[10,4,8,5,1280]{4,1,3,2,0:T(4,128)(2,1)S(1)} %bitcast.68), kind=kLoop, calls=%fused_computation.11 | loop fusion | flops 17203200 | bytes 11264000 | tf_op jit(solution)/shard_map/conv_general_dilated | solution.py:118
  103.6 4.7 %broadcast_select_fusion.1 = (bf16[2,9,1280,80]{2,3,1,0:T(8,128)(2,1)}, bf16[2,9,1280,80]{2,3,1,0:T(8,128)(2,1)}) fusion(bf16[2,9,1280,80]{2,3,1,0:T(8,128)(2,1)} %collective-permute-done.5, pred[]{:T(512)S(6)} %ne.8, bf16[1,9,1280,80]{2,3,1,0:T(8,128)(2,1)S(1)} %copy-done.1, bf16[1,9,1280,80]{2,3,1,0:T(8,128)(2,1)S(1)} %get-tuple-element.13), kind=kLoop, calls=%fused_computation.27 | loop fusion | flops 5529600 | bytes 14745601 | tf_op jit(solution)/shard_map/jit(_where)/select_n | solution.py:41
  108.3 6.8 %maximum_bitcast_fusion = bf16[9,1280,4,80]{1,3,0,2:T(8,128)(2,1)} fusion(bf16[2,9,1280,80]{2,3,1,0:T(8,128)(2,1)} %get-tuple-element.12, bf16[2,9,1280,80]{2,3,1,0:T(8,128)(2,1)} %get-tuple-element.11), kind=kLoop, calls=%fused_computation.10 | loop fusion | flops 3686400 | bytes 14745600 | tf_op jit(solution)/shard_map/transpose | solution.py:46
  115.1 3.8 %copy.75 = bf16[9,1280,4,80]{1,3,2,0:T(8,128)(2,1)S(1)} copy(bf16[9,1280,4,80]{1,3,0,2:T(8,128)(2,1)} %maximum_bitcast_fusion) | data formatting | bytes 14745600 | tf_op jit(solution)/shard_map/transpose | solution.py:46
  118.9 18.7 %select_reduce_fusion = (f32[320]{0:T(512)S(1)}, f32[320]{0:T(512)S(1)}, f32[8,32,5,320]{3,1,2,0:T(8,128)}) fusion(pred[32,5]{0,1:T(8,128)(4,1)S(1)} %copy-done.11, f32[320]{0:T(512)S(1)} %add.127, bf16[3,3,1280,320]{2,3,1,0:T(8,128)(2,1)S(1)} %bitcast.70, bf16[10,4,8,7,1280]{4,1,3,2,0:T(4,128)(2,1)} %fusion.1), kind=kOutput, calls=%fused_computation.36 | convolution fusion | flops 9440051200 | bytes 14749600 | tf_op jit(solution)/shard_map/conv_general_dilated | solution.py:118
  138.0 2.1 collective-permute-start.7
  142.0 2.2 multiply_convert_fusion
  144.6 1.6 collective-permute-start.8
  146.2 15.0 %collective-permute-done.8 = bf16[4,8,32,320]{3,1,2,0:T(8,128)(2,1)S(1)} collective-permute-done((bf16[4,8,32,320]{3,1,2,0:T(8,128)(2,1)S(1)}, bf16[4,8,32,320]{3,1,2,0:T(8,128)(2,1)S(1)}, u32[]{:S(2)}, u32[]{:S(2)}) %collective-permute-start.8) | collective-permute-done | bytes 655392 | tf_op jit(solution)/shard_map/ppermute | solution.py:16
  161.3 2.1 maximum_select_fusion.2
  163.4 2.6 collective-permute-start.9
  166.0 1.5 broadcast_select_fusion.5
  167.7 6.2 %copy.80 = bf16[3,1280,320]{2,0,1:T(4,128)(2,1)} copy(bf16[3,1280,320]{1,2,0:T(8,128)(2,1)S(1)} %bitcast.69) | data formatting | bytes 4915200 | tf_op jit(solution)/shard_map/reshape | solution.py:47
  173.9 12.0 %gather_fusion.3 = bf16[1280,3,320]{2,1,0:T(4,128)(2,1)} fusion(bf16[3,1280,320]{2,0,1:T(4,128)(2,1)} %copy.80, s32[2048]{0:T(1024)S(1)} %pad_clamp_fusion), kind=kCustom, calls=%fused_computation.3 | custom fusion | bytes 4920320 | tf_op jit(solution)/shard_map/gather | solution.py:165
  187.3 32.4 %collective-permute-done.9 = bf16[4,8,32,640]{3,1,2,0:T(8,128)(2,1)} collective-permute-done((bf16[4,8,32,640]{3,1,2,0:T(8,128)(2,1)}, bf16[4,8,32,640]{3,1,2,0:T(8,128)(2,1)}, u32[]{:S(2)}, u32[]{:S(2)}) %collective-permute-start.9) | collective-permute-done | bytes 1310752 | tf_op jit(solution)/shard_map/ppermute | solution.py:16
  219.7 1.5 copy.79
  223.3 4.4 %fusion.26 = bf16[1,4,8,32,320]{4,2,3,0,1:T(8,128)(2,1)S(1)} fusion(bf16[3,1,1280,320]{3,0,2,1:T(4,128)(2,1)S(1)} %bitcast.78, bf16[4,8,32,1280]{3,2,1,0:T(8,128)(2,1)S(1)} %bitcast.76), kind=kOutput, calls=%fused_computation.46 | convolution fusion | flops 2097479680 | bytes 5734400 | tf_op jit(solution)/shard_map/conv_general_dilated | solution.py:168
  227.7 24.8 %all_to_all.15 = bf16[1,4,8,32,320]{4,2,3,0,1:T(8,128)(2,1)S(1)} all-to-all(bf16[1,4,8,32,320]{4,2,3,0,1:T(8,128)(2,1)S(1)} %fusion.26), channel_id=1, replica_groups=mesh['rep'=4,'frame'=4,'row'=2] {'frame'}, dimensions={1} | all-to-all | bytes 1310720 | tf_op jit(solution)/shard_map/all_to_all | solution.py:177
  256.0 2.2 reshape.235
  258.2 2.3 add_add_fusion
  (89 shorter events, 24.3 us)
Async XLA Ops:
  6.5 65.0 %all-gather.2.cloned.1.call-start = ((), (), s32[]{:S(2)}) async-start(), calls=%async_computation.1 | async-start | bytes 3276800 | tf_op jit(solution)/shard_map/all_gather | solution.py:84
  7.3 59.1 %collective-permute-start.4 = (bf16[1,9,1280,80]{2,3,1,0:T(8,128)(2,1)}, bf16[1,9,1280,80]{2,3,1,0:T(8,128)(2,1)}, u32[]{:S(2)}, u32[]{:S(2)}) collective-permute-start(bf16[1,9,1280,80]{2,3,1,0:T(8,128)(2,1)} %bitcast.79), channel_id=1, source_target_pairs={{0,16},{8,24},{16,0},{24,8},{1,17},{9,25},{17,1},{25,9},{2,18},{10... | collective-permute-start | bytes 5529608 | tf_op jit(solution)/shard_map/ppermute | solution.py:39
  10.3 53.6 %collective-permute-start.10 = (bf16[1,3,1280,80]{2,3,0,1:T(8,128)(2,1)}, bf16[1,3,1280,80]{2,3,0,1:T(8,128)(2,1)S(1)}, u32[]{:S(2)}, u32[]{:S(2)}) collective-permute-start(bf16[1,3,1280,80]{2,3,0,1:T(8,128)(2,1)} %bitcast.80), channel_id=1, source_target_pairs={{0,16},{8,24},{16,0},{24,8},{1,17},{9,25},{17,1},{25,9},{2,18},{10... | collective-permute-start | bytes 1843208 | tf_op jit(solution)/shard_map/ppermute | solution.py:39
  65.0 1.3 copy-start.2
  66.3 99.7 %collective-permute-start.11 = (bf16[2,3,1280,80]{2,3,0,1:T(8,128)(2,1)}, bf16[2,3,1280,80]{2,3,0,1:T(8,128)(2,1)}, u32[]{:S(2)}, u32[]{:S(2)}) collective-permute-start(bf16[2,3,1280,80]{2,3,0,1:T(8,128)(2,1)} %pad_maximum_fusion.2), channel_id=1, source_target_pairs={{0,8},{8,0},{16,24},{24,16},{1,9},{9,1},{17,25},{25,17},{2,10},{10... | collective-permute-start | bytes 3686408 | tf_op jit(solution)/shard_map/ppermute | solution.py:39
  68.6 2.4 copy-start
  71.0 12.0 %copy-start.7 = (f32[1280]{0:T(1024)S(1)}, f32[1280]{0:T(1024)}, u32[]{:S(2)}) copy-start(f32[1280]{0:T(1024)} %param.23) | copy-start | bytes 15364
  71.0 12.0 %copy-start.8 = (f32[1280]{0:T(1024)S(1)}, f32[1280]{0:T(1024)}, u32[]{:S(2)}) copy-start(f32[1280]{0:T(1024)} %param.22) | copy-start | bytes 15364
  71.0 32.6 %collective-permute-start.5 = (bf16[2,9,1280,80]{2,3,1,0:T(8,128)(2,1)}, bf16[2,9,1280,80]{2,3,1,0:T(8,128)(2,1)}, u32[]{:S(2)}, u32[]{:S(2)}) collective-permute-start(bf16[2,9,1280,80]{2,3,1,0:T(8,128)(2,1)} %pad_maximum_fusion), channel_id=1, source_target_pairs={{0,8},{8,0},{16,24},{24,16},{1,9},{9,1},{17,25},{25,17},{2,10},{10... | collective-permute-start | bytes 11059208 | tf_op jit(solution)/shard_map/ppermute | solution.py:39
  74.2 7.2 %collective-permute-start.1 = (f32[1,32]{1,0:T(1,128)S(1)}, f32[1,32]{1,0:T(1,128)S(1)}, u32[]{:S(2)}, u32[]{:S(2)}) collective-permute-start(f32[1,32]{1,0:T(1,128)S(1)} %bitcast.81), channel_id=1, source_target_pairs={{0,1},{1,0},{2,3},{3,2},{4,5},{5,4},{6,7},{7,6},{8,9},{9,8},{10,11... | collective-permute-start | bytes 392 | tf_op jit(solution)/shard_map/ppermute | solution.py:26
  76.2 6.5 %collective-permute-start.2 = (f32[1,32]{1,0:T(1,128)S(1)}, f32[1,32]{1,0:T(1,128)S(1)}, u32[]{:S(2)}, u32[]{:S(2)}) collective-permute-start(f32[1,32]{1,0:T(1,128)S(1)} %bitcast.82), channel_id=1, source_target_pairs={{0,1},{1,0},{2,3},{3,2},{4,5},{5,4},{6,7},{7,6},{8,9},{9,8},{10,11... | collective-permute-start | bytes 392 | tf_op jit(solution)/shard_map/ppermute | solution.py:26
  77.7 10.3 %collective-permute-start = (bf16[1,4,1,32,1280]{4,3,2,0,1:T(8,128)(2,1)S(1)}, bf16[1,4,1,32,1280]{4,3,2,0,1:T(8,128)(2,1)S(1)}, u32[]{:S(2)}, u32[]{:S(2)}) collective-permute-start(bf16[1,4,1,32,1280]{4,3,2,0,1:T(8,128)(2,1)S(1)} %get-tuple-element.15), channel_id=1, source_target_pairs={{0,1},{2,3},{4,5},{6,7},{8,9},{10,11},{12,13},{14,15},{16,17},{18,... | collective-permute-start | bytes 983048 | tf_op jit(solution)/shard_map/ppermute | solution.py:89
  81.4 10.8 %collective-permute-start.3 = (bf16[1,4,1,32,1280]{4,3,2,0,1:T(8,128)(2,1)S(1)}, bf16[1,4,1,32,1280]{4,3,2,0,1:T(8,128)(2,1)}, u32[]{:S(2)}, u32[]{:S(2)}) collective-permute-start(bf16[1,4,1,32,1280]{4,3,2,0,1:T(8,128)(2,1)S(1)} %get-tuple-element.16), channel_id=1, source_target_pairs={{1,0},{3,2},{5,4},{7,6},{9,8},{11,10},{13,12},{15,14},{17,16},{19,... | collective-permute-start | bytes 983048 | tf_op jit(solution)/shard_map/ppermute | solution.py:90
  98.8 4.8 %copy-start.1 = (bf16[1,9,1280,80]{2,3,1,0:T(8,128)(2,1)S(1)}, bf16[1,9,1280,80]{2,3,1,0:T(8,128)(2,1)}, u32[]{:S(2)}) copy-start(bf16[1,9,1280,80]{2,3,1,0:T(8,128)(2,1)} %copy-done) | copy-start | bytes 5529604
  115.1 3.8 %copy-start.11 = (pred[32,5]{0,1:T(8,128)(4,1)S(1)}, pred[32,5]{0,1:T(8,128)(4,1)}, u32[]{:S(2)}) copy-start(pred[32,5]{0,1:T(8,128)(4,1)} %constant.73) | copy-start | bytes 484
  137.7 3.6 %collective-permute-start.6 = (f32[8]{0:T(128)S(1)}, f32[8]{0:T(128)S(1)}, u32[]{:S(2)}, u32[]{:S(2)}) collective-permute-start(f32[8]{0:T(128)S(1)} %reduce_sum.78), channel_id=1, source_target_pairs={{0,1},{1,0},{2,3},{3,2},{4,5},{5,4},{6,7},{7,6},{8,9},{9,8},{10,11... | collective-permute-start | bytes 104 | tf_op jit(solution)/shard_map/ppermute | solution.py:26
  138.0 3.6 %collective-permute-start.7 = (f32[8]{0:T(128)S(1)}, f32[8]{0:T(128)S(1)}, u32[]{:S(2)}, u32[]{:S(2)}) collective-permute-start(f32[8]{0:T(128)S(1)} %reduce_sum.81), channel_id=1, source_target_pairs={{0,1},{1,0},{2,3},{3,2},{4,5},{5,4},{6,7},{7,6},{8,9},{9,8},{10,11... | collective-permute-start | bytes 104 | tf_op jit(solution)/shard_map/ppermute | solution.py:26
  144.5 21.5 %copy-start.10 = (s32[1280]{0:T(1024)S(1)}, s32[1280]{0:T(1024)}, u32[]{:S(2)}) copy-start(s32[1280]{0:T(1024)} %constant.82) | copy-start | bytes 15364
  144.5 21.5 %copy-start.3 = (bf16[1,3,1280,80]{2,3,0,1:T(8,128)(2,1)S(1)}, bf16[1,3,1280,80]{2,3,0,1:T(8,128)(2,1)}, u32[]{:S(2)}) copy-start(bf16[1,3,1280,80]{2,3,0,1:T(8,128)(2,1)} %copy-done.2) | copy-start | bytes 1843204
  144.6 16.7 %collective-permute-start.8 = (bf16[4,8,32,320]{3,1,2,0:T(8,128)(2,1)S(1)}, bf16[4,8,32,320]{3,1,2,0:T(8,128)(2,1)S(1)}, u32[]{:S(2)}, u32[]{:S(2)}) collective-permute-start(bf16[4,8,32,320]{3,1,2,0:T(8,128)(2,1)S(1)} %slice_bitcast_fusion), channel_id=1, source_target_pairs={{0,2},{2,0},{4,6},{6,4},{1,3},{3,1},{5,7},{7,5},{8,10},{10,8},{12,... | collective-permute-start | bytes 1966088 | tf_op jit(solution)/shard_map/ppermute | solution.py:16
  161.3 6.2 %copy-start.4 = (bf16[4,8,32,320]{3,1,2,0:T(8,128)(2,1)}, bf16[4,8,32,320]{3,1,2,0:T(8,128)(2,1)S(1)}, u32[]{:S(2)}) copy-start(bf16[4,8,32,320]{3,1,2,0:T(8,128)(2,1)S(1)} %collective-permute-done.8) | copy-start | bytes 1966084
  163.4 56.3 %collective-permute-start.9 = (bf16[4,8,32,640]{3,1,2,0:T(8,128)(2,1)}, bf16[4,8,32,640]{3,1,2,0:T(8,128)(2,1)}, u32[]{:S(2)}, u32[]{:S(2)}) collective-permute-start(bf16[4,8,32,640]{3,1,2,0:T(8,128)(2,1)} %maximum_select_fusion.2), channel_id=1, source_target_pairs={{0,4},{2,6},{4,0},{6,2},{1,5},{3,7},{5,1},{7,3},{8,12},{10,14},{12... | collective-permute-start | bytes 3932168 | tf_op jit(solution)/shard_map/ppermute | solution.py:16
  173.9 12.2 %copy-start.5 = (bf16[4,8,32,320]{3,1,2,0:T(8,128)(2,1)S(1)}, bf16[4,8,32,320]{3,1,2,0:T(8,128)(2,1)}, u32[]{:S(2)}) copy-start(bf16[4,8,32,320]{3,1,2,0:T(8,128)(2,1)} %copy-done.4) | copy-start | bytes 1966084
  221.2 2.1 copy-start.6
  256.0 2.3 copy-start.9
Sparse Core Ops, SparseCore 0:
  8.9 57.4 all-gather.1
